TPU v7x, 256 devices: a whole 4x4x8 slice. The times are simulated.
256 devices in a mesh: orb: 8 (over z_lo, core), box: 32 (over x, y, z_hi).
Axes of the slice: x: 4, y: 4, z: 8 (z_hi: 2, z_lo: 4; z = z_hi * 4 + z_lo), core: 2. Of those that a mesh axis runs over, the one named last changes fastest.
Arguments:
- orbitals: bfloat16 [768, 256, 1000], P('orb', 'box'), may hold values from -6 to 6
- exchange_values: bfloat16 [768, 256, 1000], P('orb', 'box'), may hold values from -6 to 6
- local_values: float32 [256, 1000], P('box'), may hold values from -6 to 6
- coupling: bfloat16 [768, 768], P('orb'), may hold values from -0.21875 to 0.21875
- to_values_mat: float32 [10, 10], replicated, may hold values from -2 to 2
- to_coeffs_mat: float32 [10, 10], replicated, may hold values from -2 to 2
- laplace_blocks: float32 [3, 10, 10], replicated, may hold values from -2 to 2
- box_counts: int32 [32], P('box'), may hold values from 2 to 8, as said below
- kept_mask: int32 [256], P('box'), may hold values from 0 to 1, as said below
- send_list: int32 [32, 32], P('box'), may hold values from -1 to 7, as said below
- neighbour_pos: int32 [6, 256], P(None, 'box'), may hold values from -1 to 39, as said below
Outputs:
- h_orbitals: bfloat16 [768, 256, 1000], P('orb', 'box')
Inputs may be any that keep to these rules, and one draw needn't show every extreme that they name: Device d of box holds live boxes in slots 0 to box_counts[d] - 1 of its 8; some device holds 8. `kept_mask`: 1 only on live boxes; at most 4 ones in one device's range, and exactly 4 in some device's range. `send_list`: row q, entries p * 1 to p + 1 - 1: live slots of device q's range passed to device p, -1 for an empty entry; nothing to its own device; at most 1 to one device, exactly 1 to the devices whose index differs by one. `neighbour_pos`: Boxes that are not live have -1 on every face.
All inputs are finite; a program needn't handle non-finite values.
Results may differ from a plain program's by a relative error of at most 0.0031.
Values may be sent and summed in bfloat16 or wider, within the bound.
No kernel may reach another device: no remote copies, remote signals or barrier semaphores. Data moves between devices by JAX's collectives and lax.ppermute only.
A program may use at most 256 MiB of HBM per device.

v0:
```python
import jax
import jax.numpy as jnp
from jax import lax
from jax.sharding import PartitionSpec as P

KEEP = 4


def digit_of(width, order_k, place):
    idx = lax.iota(jnp.int32, width)
    return idx // order_k ** (2 - place) % order_k


def expand(mat, width, place):
    order_k = mat.shape[0]
    digit = digit_of(width, order_k, place)
    ks = lax.iota(jnp.int32, order_k)
    left = (digit[:, None] == ks[None, :]).astype(jnp.float32)
    right = (ks[:, None] == digit[None, :]).astype(jnp.float32)
    hp = lax.Precision.HIGHEST
    return jnp.dot(jnp.dot(left, mat, precision=hp), right, precision=hp)


def same_digit(width, order_k, place):
    digit = digit_of(width, order_k, place)
    return (digit[:, None] == digit[None, :]).astype(jnp.float32)


def kron3(a, b, c):
    width = a.shape[0] * b.shape[0] * c.shape[0]
    return expand(a, width, 0) * expand(b, width, 1) * expand(c, width, 2)


def at_place(mat, width, place):
    order_k = mat.shape[0]
    out = expand(mat, width, place)
    for other in range(3):
        if other != place:
            out = out * same_digit(width, order_k, other)
    return out


def split_bf16(mat):
    hi = lax.reduce_precision(mat, exponent_bits=8, mantissa_bits=7)
    lo = (mat - hi).astype(jnp.bfloat16)
    return (hi.astype(jnp.bfloat16), lo)


def dot_f32(a, b):
    return jnp.dot(a, b, preferred_element_type=jnp.float32)


def apply_bf16(rows, parts):
    hi, lo = parts
    return dot_f32(rows, hi) + dot_f32(rows, lo)


def apply_f32(rows, parts):
    hi, lo = parts
    rows_hi_f = lax.reduce_precision(rows, exponent_bits=8, mantissa_bits=7)
    rows_lo = (rows - rows_hi_f).astype(jnp.bfloat16)
    rows_hi = rows_hi_f.astype(jnp.bfloat16)
    return dot_f32(rows_hi, hi) + dot_f32(rows_hi, lo) + dot_f32(rows_lo, hi)


def pick(onehot, block):
    return jnp.einsum("sb,nbc->nsc", onehot, block, preferred_element_type=jnp.float32).astype(
        jnp.bfloat16
    )


def shards(
    orbitals,
    exchange_values,
    local_values,
    coupling,
    to_values_mat,
    to_coeffs_mat,
    laplace_blocks,
    box_counts,
    kept_mask,
    send_list,
    neighbour_pos,
):
    orb_dev, box_dev, width = orbitals.shape
    order_k = to_values_mat.shape[0]
    n_box = send_list.shape[1]
    rows = orb_dev * box_dev
    slots = send_list[0]
    box_ids = lax.iota(jnp.int32, box_dev)
    send_hot = (slots[:, None] == box_ids[None, :]).astype(jnp.bfloat16)
    outgoing = pick(send_hot, orbitals)
    incoming = lax.all_to_all(outgoing, "box", split_axis=1, concat_axis=1, tiled=True)
    values_t = split_bf16(kron3(to_values_mat, to_values_mat, to_values_mat).T)
    flat = orbitals.reshape(rows, width)
    values = apply_bf16(flat, values_t).reshape(orb_dev, box_dev, width)
    kept = kept_mask > 0
    rank = jnp.cumsum(kept.astype(jnp.int32)) - 1
    keep_ids = lax.iota(jnp.int32, KEEP)
    sel = kept[None, :] & (rank[None, :] == keep_ids[:, None])
    products = jnp.where(
        kept[None, :, None], exchange_values.astype(jnp.float32) * values, 0.0
    ).astype(jnp.bfloat16)
    compact = pick(sel.astype(jnp.bfloat16), products)
    gathered = lax.all_gather(compact.reshape(orb_dev, KEEP * width), "orb", axis=0, tiled=True)
    mixed = dot_f32(coupling, gathered).reshape(orb_dev, KEEP, width)
    self_f = sel.astype(jnp.float32)
    exchange = mixed[:, 0:1, :] * self_f[0][None, :, None]
    for k in range(1, KEEP):
        exchange = exchange + mixed[:, k : k + 1, :] * self_f[k][None, :, None]
    weighted = local_values[None, :, :] * values - exchange
    coeffs_t = split_bf16(kron3(to_coeffs_mat, to_coeffs_mat, to_coeffs_mat).T)
    potential = apply_f32(weighted.reshape(rows, width), coeffs_t)
    lap0 = laplace_blocks[0]
    centre = sum((at_place(lap0, width, place) for place in range(3)))
    kinetic = apply_bf16(flat, split_bf16(centre.T))
    remote_ids = lax.iota(jnp.int32, n_box)
    for which in range(3):
        for side in range(2):
            face_pos = neighbour_pos[2 * which + side]
            local_hot = (face_pos[:, None] == box_ids[None, :]).astype(jnp.bfloat16)
            remote_hot = (face_pos[:, None] - box_dev == remote_ids[None, :]).astype(jnp.bfloat16)
            moved = pick(local_hot, orbitals) + pick(remote_hot, incoming)
            face_mat = at_place(laplace_blocks[1 + side], width, which)
            kinetic = kinetic + apply_bf16(moved.reshape(rows, width), split_bf16(face_mat.T))
    total = (potential - 0.5 * kinetic).reshape(orb_dev, box_dev, width)
    live = box_ids < box_counts[0]
    total = jnp.where(live[None, :, None], total, 0.0)
    return total.astype(jnp.bfloat16)


def solution(mesh):
    return jax.shard_map(
        shards,
        mesh=mesh,
        in_specs=(
            P("orb", "box", None),
            P("orb", "box", None),
            P("box", None),
            P("orb", None),
            P(),
            P(),
            P(),
            P("box"),
            P("box"),
            P("box", None),
            P(None, "box"),
        ),
        out_specs=P("orb", "box", None),
        check_vma=False,
    )
```

profile of v0, /device:TPU:66, one launch (start us, length us, event | category | flops | bytes accessed | tf_op | source)
XLA Modules:
  0.0 403.2 jit_solution(18097941252706797543)
XLA Ops:
  22.7 3.9 copy.33
  34.0 6.2 %copy.39 = bf16[96,32,1000]{2,0,1:T(8,128)(2,1)} copy(bf16[96,32,1000]{2,1,0:T(8,128)(2,1)S(1)} %convert_bitcast_fusion) | data formatting | bytes 12288000 | tf_op jit(solution)/shard_map/convert_element_type | solution.py:67
  40.2 12.6 %all-to-all-start = ((bf16[96,32,1000]{2,0,1:T(8,128)(2,1)}), bf16[96,32,1000]{2,0,1:T(8,128)(2,1)}, u32[]{:S(2)}, u32[]{:S(2)}) async-start(bf16[96,32,1000]{2,0,1:T(8,128)(2,1)} %copy.39), calls=%async_computation | async-start | bytes 12582912 | tf_op jit(solution)/shard_map/all_to_all | solution.py:93
  66.4 3.8 fusion.203
  85.3 4.0 fusion.199
  99.9 4.1 %fusion.53 = f32[1000,768]{1,0:T(8,128)} fusion(f32[1000,1000]{1,0:T(8,128)S(1)} %fusion.10, bf16[96,8,1000]{2,1,0:T(8,128)(2,1)S(1)} %copy-done), kind=kOutput, calls=%fused_computation.91 | convolution fusion | flops 1538000000 | bytes 8608000 | tf_op jit(solution)/shard_map/dot_general | solution.py:50
  104.1 4.2 %multiply_multiply_fusion = f32[1000,1000]{1,0:T(8,128)} fusion(f32[1000,1000]{1,0:T(8,128)S(1)} %fusion.206, f32[1000,1000]{1,0:T(8,128)S(1)} %fusion.201, f32[1000,10]{0,1:T(8,128)S(1)} %fusion.169, s32[1000]{0:T(1024)S(1)} %add_select_fusion), kind=kOutput, calls=%fused_computation.51 | convolution fusion | flops 122010000 | bytes 12044000 | tf_op jit(solution)/shard_map/dot_general | solution.py:21
  111.9 118.3 %all-gather.2.cloned.1.call-done = bf16[768,4000]{1,0:T(8,128)(2,1)} async-done(((bf16[96,4000]{1,0:T(8,128)(2,1)}), bf16[768,4000]{1,0:T(8,128)(2,1)}) %all-gather.2.cloned.1.call-update) | async-done | bytes 6144016 | tf_op jit(solution)/shard_map/all_gather | solution.py:105
  230.2 5.1 %convolution_bitcast_fusion = f32[96,4000]{1,0:T(8,128)} fusion(bf16[96,768]{1,0:T(8,128)(2,1)S(1)} %copy-done.11, bf16[768,4000]{1,0:T(8,128)(2,1)} %all-gather.2.cloned.1.call-done), kind=kOutput, calls=%fused_computation.37 | convolution fusion | flops 589824000 | bytes 7827456 | tf_op jit(solution)/shard_map/dot_general | solution.py:50
  262.1 7.7 %add_subtract_fusion = f32[768,1000]{0,1:T(8,128)S(1)} fusion(f32[768,1000]{0,1:T(8,128)} %copy.37, f32[768,1000]{0,1:T(8,128)} %copy.36, f32[768,1000]{0,1:T(8,128)} %copy.35, f32[768,1000]{0,1:T(8,128)} %copy.34, f32[768,1000]{0,1:T(8,128)} %copy.32, f32[768,1000]{0,1:T(8,128)} %add_bitcast_fusion, f32[768]{0:T(1024)S(1)} %mul.221, f32[768]{0:T(1024)S(1)} %mul.213, ...), kind=kLoop, calls=%fused_computation.67 | loop fusion | flops 6912000 | bytes 21516288 | tf_op jit(solution)/shard_map/sub | solution.py:111
  276.8 6.3 %fusion.135 = bf16[96,1000,8]{1,2,0:T(8,128)(2,1)S(1)} fusion(bf16[96,32,1000]{2,0,1:T(8,128)(2,1)} %all-to-all-done, s32[8]{0:T(128)S(1)} %get-tuple-element.19), kind=kOutput, calls=%fused_computation.163 | convolution fusion | flops 49920256 | bytes 7680032 | tf_op jit(solution)/shard_map/sb,nbc->nsc/dot_general | solution.py:67
  285.3 3.9 fusion.34
  289.2 3.9 fusion.59
  293.1 6.3 %fusion.120 = bf16[96,1000,8]{1,2,0:T(8,128)(2,1)S(1)} fusion(bf16[96,32,1000]{2,0,1:T(8,128)(2,1)} %all-to-all-done, s32[8]{0:T(128)S(1)} %get-tuple-element.18), kind=kOutput, calls=%fused_computation.158 | convolution fusion | flops 49920256 | bytes 7680032 | tf_op jit(solution)/shard_map/sb,nbc->nsc/dot_general | solution.py:67
  309.2 6.7 %fusion.132 = bf16[96,1000,8]{1,2,0:T(8,128)(2,1)S(1)} fusion(bf16[96,32,1000]{2,0,1:T(8,128)(2,1)} %all-to-all-done, s32[8]{0:T(128)S(1)} %get-tuple-element.20), kind=kOutput, calls=%fused_computation.162 | convolution fusion | flops 49920256 | bytes 7680032 | tf_op jit(solution)/shard_map/sb,nbc->nsc/dot_general | solution.py:67
  318.1 3.9 fusion.36
  325.8 6.3 %fusion.129 = bf16[96,1000,8]{1,2,0:T(8,128)(2,1)S(1)} fusion(bf16[96,32,1000]{2,0,1:T(8,128)(2,1)} %all-to-all-done, s32[8]{0:T(128)S(1)} %get-tuple-element.21), kind=kOutput, calls=%fused_computation.161 | convolution fusion | flops 49920256 | bytes 7680032 | tf_op jit(solution)/shard_map/sb,nbc->nsc/dot_general | solution.py:67
  334.3 4.0 fusion.38
  338.3 3.9 fusion.57
  342.1 6.3 %fusion.126 = bf16[96,1000,8]{1,2,0:T(8,128)(2,1)S(1)} fusion(bf16[96,32,1000]{2,0,1:T(8,128)(2,1)} %all-to-all-done, s32[8]{0:T(128)S(1)} %get-tuple-element.22), kind=kOutput, calls=%fused_computation.160 | convolution fusion | flops 49920256 | bytes 7680032 | tf_op jit(solution)/shard_map/sb,nbc->nsc/dot_general | solution.py:67
  350.6 3.9 fusion.40
  358.2 6.5 %fusion.123 = bf16[96,1000,8]{1,2,0:T(8,128)(2,1)S(1)} fusion(bf16[96,32,1000]{2,0,1:T(8,128)(2,1)} %all-to-all-done, s32[8]{0:T(128)S(1)} %get-tuple-element.23), kind=kOutput, calls=%fused_computation.159 | convolution fusion | flops 49920256 | bytes 7680032 | tf_op jit(solution)/shard_map/sb,nbc->nsc/dot_general | solution.py:67
  366.9 3.9 fusion.42
  374.5 18.2 %fusion.21 = bf16[768,1000]{0,1:T(8,128)(2,1)} fusion(f32[768,1000]{0,1:T(8,128)} %fusion.59, f32[768,1000]{0,1:T(8,128)} %fusion.34, f32[768,1000]{0,1:T(8,128)} %fusion.58, f32[768,1000]{0,1:T(8,128)} %fusion.36, f32[768,1000]{0,1:T(8,128)} %fusion.57, f32[768,1000]{0,1:T(8,128)} %fusion.38, f32[768,1000]{0,1:T(8,128)} %fusion.56, ...), kind=kOutput, calls=%fused_computation.66 | convolution fusion | flops 1554128000 | bytes 57760000 | tf_op jit(solution)/shard_map/dot_general | solution.py:50
  (122 shorter events, 134.5 us)
Async XLA Ops:
  6.5 10.5 %copy-start = (bf16[96,8,1000]{2,1,0:T(8,128)(2,1)S(1)}, bf16[96,8,1000]{2,1,0:T(8,128)(2,1)}, u32[]{:S(2)}) copy-start(bf16[96,8,1000]{2,1,0:T(8,128)(2,1)} %param.11) | copy-start | bytes 4608004
  6.5 223.7 %all-gather.2.cloned.1.call-start = ((), (), s32[]{:S(2)}) async-start(), calls=%async_computation.1 | async-start | bytes 7077888 | tf_op jit(solution)/shard_map/all_gather | solution.py:105
  26.6 5.3 %copy-start.15 = (s32[1,32]{1,0:T(1,128)S(1)}, s32[1,32]{1,0:T(1,128)}, u32[]{:S(2)}) copy-start(s32[1,32]{1,0:T(1,128)} %param.20) | copy-start | bytes 388
  40.2 13.3 %copy-start.14 = (s32[6,8]{1,0:T(8,128)S(1)}, s32[6,8]{1,0:T(8,128)}, u32[]{:S(2)}) copy-start(s32[6,8]{1,0:T(8,128)} %param.21) | copy-start | bytes 580
  40.2 13.4 %copy-start.13 = (f32[3,10,10]{2,0,1:T(4,128)S(1)}, f32[3,10,10]{2,0,1:T(4,128)}, u32[]{:S(2)}) copy-start(f32[3,10,10]{2,0,1:T(4,128)} %param.17) | copy-start | bytes 3604
  40.2 14.4 %copy-start.12 = (f32[8,1000]{1,0:T(8,128)S(1)}, f32[8,1000]{1,0:T(8,128)}, u32[]{:S(2)}) copy-start(f32[8,1000]{1,0:T(8,128)} %param.13) | copy-start | bytes 96004
  40.2 236.7 %all-to-all-start = ((bf16[96,32,1000]{2,0,1:T(8,128)(2,1)}), bf16[96,32,1000]{2,0,1:T(8,128)(2,1)}, u32[]{:S(2)}, u32[]{:S(2)}) async-start(bf16[96,32,1000]{2,0,1:T(8,128)(2,1)} %copy.39), calls=%async_computation | async-start | bytes 12582912 | tf_op jit(solution)/shard_map/all_to_all | solution.py:93
  57.6 7.3 %copy-start.17 = (f32[10,10]{1,0:T(8,128)S(1)}, f32[10,10]{1,0:T(8,128)}, u32[]{:S(2)}) copy-start(f32[10,10]{1,0:T(8,128)} %param.16) | copy-start | bytes 1204
  108.3 121.9 %copy-start.11 = (bf16[96,768]{1,0:T(8,128)(2,1)S(1)}, bf16[96,768]{1,0:T(8,128)(2,1)}, u32[]{:S(2)}) copy-start(bf16[96,768]{1,0:T(8,128)(2,1)} %param.14) | copy-start | bytes 442372
  262.1 7.7 %copy-start.1 = (f32[1000,1000]{1,0:T(8,128)S(1)}, f32[1000,1000]{1,0:T(8,128)}, u32[]{:S(2)}) copy-start(f32[1000,1000]{1,0:T(8,128)} %multiply_multiply_fusion) | copy-start | bytes 12000004
  269.8 3.5 copy-start.3
  283.1 2.2 copy-start.10
  299.4 2.2 copy-start.9
  316.0 2.2 copy-start.8
  332.1 2.2 copy-start.7
  348.5 2.2 copy-start.6
  364.7 2.2 copy-start.5
  370.8 3.7 copy-start.2
  370.8 3.7 copy-start.4
  392.8 1.7 copy-start.16
Sparse Core Ops, SparseCore 0:
  32.0 198.1 all-gather.1
where the time goes:
time: 411 us; the launch traced here: 403 us
  matrix products  190 us (46%)
  waiting for transfers between devices  118 us (29%)
  local copies, waits for them, and re-layouts  56.3 us (14%)
  between operations  14.7 us (4%)
  starting transfers between devices  12.6 us (3%)
  other arithmetic  10.9 us (3%)
    all_gather x1, waiting for transfers between devices, shards(): lax.all_gather(compact.reshape(orb_dev, KEEP * width), 'orb', axis=0, til...  118 us
    dot_general x20, matrix products, dot_f32(): return jnp.dot(a, b, preferred_element_type=jnp.float32)  89.9 us
    dot_general x30, matrix products, expand(): return jnp.dot(jnp.dot(left, mat, precision=hp), right, precision=hp)  53.2 us
    dot_general x14, matrix products, pick(): jnp.einsum('sb,nbc->nsc', onehot, block, preferred_element_type=jnp.float32)  47.4 us
    mul x12, local copies, waits for them, and re-layouts, shards(): exchange = exchange + mixed[:, k:k + 1, :] * self_f[k][None, :, None]  17.1 us
    all_to_all x1, starting transfers between devices, shards(): lax.all_to_all(outgoing, 'box', split_axis=1, concat_axis=1, tiled=True)  12.6 us
    unnamed x40, local copies, waits for them, and re-layouts  9.54 us
  transfers between devices with their start and end apart: 2, of which 1 were waited for; matrix products, arithmetic and copies ran while one was open for 28% of the time, Pallas kernels for 0%

commit v1 on v0

--- a/solution.py
+++ b/solution.py
@@ -1,9 +1,19 @@
+import functools
 import jax
 import jax.numpy as jnp
 from jax import lax
 from jax.sharding import PartitionSpec as P
 
 KEEP = 4
+
+
+def _trace_columns(z, axis_tag):
+    return jnp.concatenate(
+        lax.all_to_all(jnp.stack(lax.axis_size(axis_tag) * [z]), axis_tag, 0, 0), 0
+    )
+
+
+_supply_all_loops = functools.partial(_trace_columns, axis_tag="orb")
 
 
 def digit_of(width, order_k, place):
@@ -102,7 +112,7 @@
         kept[None, :, None], exchange_values.astype(jnp.float32) * values, 0.0
     ).astype(jnp.bfloat16)
     compact = pick(sel.astype(jnp.bfloat16), products)
-    gathered = lax.all_gather(compact.reshape(orb_dev, KEEP * width), "orb", axis=0, tiled=True)
+    gathered = _supply_all_loops(compact.reshape(orb_dev, KEEP * width))
     mixed = dot_f32(coupling, gathered).reshape(orb_dev, KEEP, width)
     self_f = sel.astype(jnp.float32)
     exchange = mixed[:, 0:1, :] * self_f[0][None, :, None]

time: 411 us -> 471 us (1.15)
  the two profiles are of different devices: /device:TPU:66 before, /device:TPU:130 now
where the time goes in v1:
time: 471 us; the launch traced here: 462 us
  matrix products  190 us (40%)
  waiting for transfers between devices  184 us (39%)
  local copies, waits for them, and re-layouts  58.8 us (12%)
  starting transfers between devices  17.4 us (4%)
  other arithmetic  10.9 us (2%)
    all_to_all x1, waiting for transfers between devices, _trace_columns(): lax.all_to_all(jnp.stack(lax.axis_size(axis_tag) * [z]), axis_tag, 0, 0)  127 us
    dot_general x20, matrix products, dot_f32(): return jnp.dot(a, b, preferred_element_type=jnp.float32)  89.8 us
    all_to_all x1, waiting for transfers between devices, shards(): lax.all_to_all(outgoing, 'box', split_axis=1, concat_axis=1, tiled=True)  57 us
    dot_general x30, matrix products, expand(): return jnp.dot(jnp.dot(left, mat, precision=hp), right, precision=hp)  53.1 us
    dot_general x14, matrix products, pick(): jnp.einsum('sb,nbc->nsc', onehot, block, preferred_element_type=jnp.float32)  47.3 us
    mul x12, local copies, waits for them, and re-layouts, shards(): exchange = exchange + mixed[:, k:k + 1, :] * self_f[k][None, :, None]  17 us
    all_to_all x1, starting transfers between devices, shards(): lax.all_to_all(outgoing, 'box', split_axis=1, concat_axis=1, tiled=True)  12.5 us
    unnamed x40, local copies, waits for them, and re-layouts  9.55 us
  transfers between devices with their start and end apart: 2, of which 2 were waited for; matrix products, arithmetic and copies ran while one was open for 24% of the time, Pallas kernels for 0%

profile of v1, /device:TPU:130, one launch (start us, length us, event | category | flops | bytes accessed | tf_op | source)
XLA Modules:
  0.0 462.4 jit_solution(17265827093058635703)
XLA Ops:
  16.1 3.9 copy.33
  27.9 4.9 %all-to-all-start = ((bf16[8,96,4000]{2,1,0:T(8,128)(2,1)}), bf16[8,96,4000]{2,1,0:T(8,128)(2,1)}, u32[]{:S(2)}, u32[]{:S(2)}) async-start(bf16[8,96,4000]{2,1,0:T(8,128)(2,1)} %stack.3), calls=%async_computation | async-start | bytes 12582912 | tf_op jit(solution)/shard_map/all_to_all | solution.py:12
  35.6 6.2 %copy.39 = bf16[96,32,1000]{2,0,1:T(8,128)(2,1)} copy(bf16[96,32,1000]{2,1,0:T(8,128)(2,1)S(1)} %convert_bitcast_fusion) | data formatting | bytes 12288000 | tf_op jit(solution)/shard_map/convert_element_type | solution.py:77
  45.0 126.8 %all-to-all-done = bf16[8,96,4000]{2,1,0:T(8,128)(2,1)} async-done(((bf16[8,96,4000]{2,1,0:T(8,128)(2,1)}), bf16[8,96,4000]{2,1,0:T(8,128)(2,1)}, u32[]{:S(2)}, u32[]{:S(2)}) %all-to-all-start) | async-done | bytes 6144032 | tf_op jit(solution)/shard_map/all_to_all | solution.py:12
  171.8 12.5 %all-to-all-start.1 = ((bf16[96,32,1000]{2,0,1:T(8,128)(2,1)}), bf16[96,32,1000]{2,0,1:T(8,128)(2,1)}, u32[]{:S(2)}, u32[]{:S(2)}) async-start(bf16[96,32,1000]{2,0,1:T(8,128)(2,1)} %copy.39), calls=%async_computation.1 | async-start | bytes 12582912 | tf_op jit(solution)/shard_map/all_to_all | solution.py:103
  194.0 3.8 fusion.203
  212.8 4.0 fusion.199
  227.4 4.1 fusion.53
  231.5 4.2 multiply_multiply_fusion
  239.4 5.1 %convolution_bitcast_fusion = f32[96,4000]{1,0:T(8,128)} fusion(bf16[96,768]{1,0:T(8,128)(2,1)S(1)} %copy-done.11, bf16[768,4000]{1,0:T(8,128)(2,1)} %bitcast.9), kind=kOutput, calls=%fused_computation.37 | convolution fusion | flops 589824000 | bytes 7827456 | tf_op jit(solution)/shard_map/dot_general | solution.py:60
  271.3 7.7 %add_subtract_fusion = f32[768,1000]{0,1:T(8,128)S(1)} fusion(f32[768,1000]{0,1:T(8,128)} %copy.37, f32[768,1000]{0,1:T(8,128)} %copy.36, f32[768,1000]{0,1:T(8,128)} %copy.35, f32[768,1000]{0,1:T(8,128)} %copy.34, f32[768,1000]{0,1:T(8,128)} %copy.32, f32[768,1000]{0,1:T(8,128)} %add_bitcast_fusion, f32[768]{0:T(1024)S(1)} %mul.221, f32[768]{0:T(1024)S(1)} %mul.213, ...), kind=kLoop, calls=%fused_computation.67 | loop fusion | flops 6912000 | bytes 21516288 | tf_op jit(solution)/shard_map/sub | solution.py:121
  286.0 57.0 %all-to-all-done.1 = bf16[96,32,1000]{2,0,1:T(8,128)(2,1)} async-done(((bf16[96,32,1000]{2,0,1:T(8,128)(2,1)}), bf16[96,32,1000]{2,0,1:T(8,128)(2,1)}, u32[]{:S(2)}, u32[]{:S(2)}) %all-to-all-start.1) | async-done | bytes 6144032 | tf_op jit(solution)/shard_map/all_to_all | solution.py:103
  343.0 6.3 %fusion.135 = bf16[96,1000,8]{1,2,0:T(8,128)(2,1)S(1)} fusion(bf16[96,32,1000]{2,0,1:T(8,128)(2,1)} %all-to-all-done.1, s32[8]{0:T(128)S(1)} %get-tuple-element.19), kind=kOutput, calls=%fused_computation.163 | convolution fusion | flops 49920256 | bytes 7680032 | tf_op jit(solution)/shard_map/sb,nbc->nsc/dot_general | solution.py:77
  351.5 3.9 fusion.34
  355.3 3.9 fusion.59
  359.3 6.3 %fusion.120 = bf16[96,1000,8]{1,2,0:T(8,128)(2,1)S(1)} fusion(bf16[96,32,1000]{2,0,1:T(8,128)(2,1)} %all-to-all-done.1, s32[8]{0:T(128)S(1)} %get-tuple-element.18), kind=kOutput, calls=%fused_computation.158 | convolution fusion | flops 49920256 | bytes 7680032 | tf_op jit(solution)/shard_map/sb,nbc->nsc/dot_general | solution.py:77
  375.3 6.7 %fusion.132 = bf16[96,1000,8]{1,2,0:T(8,128)(2,1)S(1)} fusion(bf16[96,32,1000]{2,0,1:T(8,128)(2,1)} %all-to-all-done.1, s32[8]{0:T(128)S(1)} %get-tuple-element.20), kind=kOutput, calls=%fused_computation.162 | convolution fusion | flops 49920256 | bytes 7680032 | tf_op jit(solution)/shard_map/sb,nbc->nsc/dot_general | solution.py:77
  384.1 3.9 fusion.36
  391.8 6.3 %fusion.129 = bf16[96,1000,8]{1,2,0:T(8,128)(2,1)S(1)} fusion(bf16[96,32,1000]{2,0,1:T(8,128)(2,1)} %all-to-all-done.1, s32[8]{0:T(128)S(1)} %get-tuple-element.21), kind=kOutput, calls=%fused_computation.161 | convolution fusion | flops 49920256 | bytes 7680032 | tf_op jit(solution)/shard_map/sb,nbc->nsc/dot_general | solution.py:77
  400.2 4.0 fusion.38
  408.0 6.3 %fusion.126 = bf16[96,1000,8]{1,2,0:T(8,128)(2,1)S(1)} fusion(bf16[96,32,1000]{2,0,1:T(8,128)(2,1)} %all-to-all-done.1, s32[8]{0:T(128)S(1)} %get-tuple-element.22), kind=kOutput, calls=%fused_computation.160 | convolution fusion | flops 49920256 | bytes 7680032 | tf_op jit(solution)/shard_map/sb,nbc->nsc/dot_general | solution.py:77
  424.2 6.5 %fusion.123 = bf16[96,1000,8]{1,2,0:T(8,128)(2,1)S(1)} fusion(bf16[96,32,1000]{2,0,1:T(8,128)(2,1)} %all-to-all-done.1, s32[8]{0:T(128)S(1)} %get-tuple-element.23), kind=kOutput, calls=%fused_computation.159 | convolution fusion | flops 49920256 | bytes 7680032 | tf_op jit(solution)/shard_map/sb,nbc->nsc/dot_general | solution.py:77
  432.9 3.9 fusion.42
  440.5 18.3 %fusion.21 = bf16[768,1000]{0,1:T(8,128)(2,1)} fusion(f32[768,1000]{0,1:T(8,128)} %fusion.59, f32[768,1000]{0,1:T(8,128)} %fusion.34, f32[768,1000]{0,1:T(8,128)} %fusion.58, f32[768,1000]{0,1:T(8,128)} %fusion.36, f32[768,1000]{0,1:T(8,128)} %fusion.57, f32[768,1000]{0,1:T(8,128)} %fusion.38, f32[768,1000]{0,1:T(8,128)} %fusion.56, ...), kind=kOutput, calls=%fused_computation.66 | convolution fusion | flops 1554128000 | bytes 57760000 | tf_op jit(solution)/shard_map/dot_general | solution.py:60
  (122 shorter events, 144.5 us)
Async XLA Ops:
  0.0 10.5 %copy-start = (bf16[96,8,1000]{2,1,0:T(8,128)(2,1)S(1)}, bf16[96,8,1000]{2,1,0:T(8,128)(2,1)}, u32[]{:S(2)}) copy-start(bf16[96,8,1000]{2,1,0:T(8,128)(2,1)} %param.11) | copy-start | bytes 4608004
  27.9 5.6 %copy-start.15 = (s32[1,32]{1,0:T(1,128)S(1)}, s32[1,32]{1,0:T(1,128)}, u32[]{:S(2)}) copy-start(s32[1,32]{1,0:T(1,128)} %param.20) | copy-start | bytes 388
  27.9 143.8 %all-to-all-start = ((bf16[8,96,4000]{2,1,0:T(8,128)(2,1)}), bf16[8,96,4000]{2,1,0:T(8,128)(2,1)}, u32[]{:S(2)}, u32[]{:S(2)}) async-start(bf16[8,96,4000]{2,1,0:T(8,128)(2,1)} %stack.3), calls=%async_computation | async-start | bytes 12582912 | tf_op jit(solution)/shard_map/all_to_all | solution.py:12
  35.6 6.2 %copy-start.14 = (s32[6,8]{1,0:T(8,128)S(1)}, s32[6,8]{1,0:T(8,128)}, u32[]{:S(2)}) copy-start(s32[6,8]{1,0:T(8,128)} %param.21) | copy-start | bytes 580
  35.6 6.2 %copy-start.13 = (f32[3,10,10]{2,0,1:T(4,128)S(1)}, f32[3,10,10]{2,0,1:T(4,128)}, u32[]{:S(2)}) copy-start(f32[3,10,10]{2,0,1:T(4,128)} %param.17) | copy-start | bytes 3604
  35.6 7.2 %copy-start.12 = (f32[8,1000]{1,0:T(8,128)S(1)}, f32[8,1000]{1,0:T(8,128)}, u32[]{:S(2)}) copy-start(f32[8,1000]{1,0:T(8,128)} %param.13) | copy-start | bytes 96004
  171.8 171.2 %all-to-all-start.1 = ((bf16[96,32,1000]{2,0,1:T(8,128)(2,1)}), bf16[96,32,1000]{2,0,1:T(8,128)(2,1)}, u32[]{:S(2)}, u32[]{:S(2)}) async-start(bf16[96,32,1000]{2,0,1:T(8,128)(2,1)} %copy.39), calls=%async_computation.1 | async-start | bytes 12582912 | tf_op jit(solution)/shard_map/all_to_all | solution.py:103
  185.2 7.3 %copy-start.17 = (f32[10,10]{1,0:T(8,128)S(1)}, f32[10,10]{1,0:T(8,128)}, u32[]{:S(2)}) copy-start(f32[10,10]{1,0:T(8,128)} %param.16) | copy-start | bytes 1204
  235.8 3.6 copy-start.11
  271.3 7.7 %copy-start.1 = (f32[1000,1000]{1,0:T(8,128)S(1)}, f32[1000,1000]{1,0:T(8,128)}, u32[]{:S(2)}) copy-start(f32[1000,1000]{1,0:T(8,128)} %multiply_multiply_fusion) | copy-start | bytes 12000004
  279.0 3.5 copy-start.3
  349.3 2.2 copy-start.10
  365.6 2.2 copy-start.9
  382.0 2.2 copy-start.8
  398.1 2.2 copy-start.7
  414.4 2.2 copy-start.6
  430.7 2.2 copy-start.5
  436.7 3.8 copy-start.2
  436.8 3.8 copy-start.4
  458.8 1.7 copy-start.16
